TPU v7x, 128 devices: a whole 4x4x4 slice. The times are simulated.
128 devices in a mesh: row: 32 (over y, z_lo, x), col: 4 (over z_hi, core).
Axes of the slice: x: 4, y: 4, z: 4 (z_hi: 2, z_lo: 2; z = z_hi * 2 + z_lo), core: 2. Of those that a mesh axis runs over, the one named last changes fastest.
Arguments:
- ratings: bfloat16 [4, 262144, 512], P(None, ('row', 'col'))
- tile_mask: int32 [4, 2048, 4], P(None, ('row', 'col')), may hold values from 0 to 1, as said below
- tile_counts: int32 [128], replicated, may hold values from 1 to 16, as said below
- users: float32 [131072, 128], P(('row', 'col')), may hold values from -2 to 2
- user_accum: float32 [131072, 128], P(('row', 'col')), may hold values from 0.05 to 0.5
- items: float32 [65536, 128], P(('row', 'col')), may hold values from -2 to 2
- item_accum: float32 [65536, 128], P(('row', 'col')), may hold values from 0.05 to 0.5
Outputs:
- users_out: float32 [131072, 128], P(('row', 'col'))
- user_accum_out: float32 [131072, 128], P(('row', 'col'))
- items_out: float32 [65536, 128], P(('row', 'col'))
- item_accum_out: float32 [65536, 128], P(('row', 'col'))
- losses: float32 [4], replicated
Inputs may be any that keep to these rules, and one draw needn't show every extreme that they name: Each group of 4 positions has tile_counts summing to 32, and exactly one position of each group, not always the same, owns 2 * 8 tiles. `tile_mask`: in each stratum, the first slot's first item tile of every position is 1.
All inputs are finite; a program needn't handle non-finite values.
Results may differ from a plain program's by a relative error of at most 0.0025.
Values sent between devices are 32-bit elements; how exact they have to be, the bound alone decides.
No kernel may reach another device: no remote copies, remote signals or barrier semaphores. Data moves between devices by JAX's collectives and lax.ppermute only.
A program may use at most 64 MiB of HBM per device.

v0:
```python
import jax
import jax.numpy as jnp
from jax import lax
from jax.sharding import PartitionSpec as P

TILE = 128
UT = 8
STEPS = 3
ridge_weight = 0.02
step_rate = 0.05


def passed_along(value, axis, steps):
    count = lax.axis_size(axis)
    pairs = [(source, (source + steps) % count) for source in range(count)]
    return lax.ppermute(value, axis, pairs)


def update(user_fac, user_acc, item_fac, item_acc, rating_block, live_tiles):
    tile_size = user_fac.shape[0] // live_tiles.shape[0]
    user_half = user_fac.astype(jnp.bfloat16)
    item_half = item_fac.astype(jnp.bfloat16)
    predicted = lax.dot_general(
        user_half, item_half, (((1,), (1,)), ((), ())), preferred_element_type=jnp.float32
    )
    residue = predicted - rating_block.astype(jnp.float32)
    masked = (
        residue.reshape(live_tiles.shape[0], tile_size, live_tiles.shape[1], tile_size)
        * live_tiles[:, None, :, None]
    ).reshape(residue.shape)
    sq_error = jnp.sum(masked * residue)
    err_half = masked.astype(jnp.bfloat16)
    grad_user = (
        jnp.dot(err_half, item_half, preferred_element_type=jnp.float32)
        * float(item_fac.shape[0]) ** (-0.5)
        + ridge_weight * user_fac
    )
    grad_item = (
        lax.dot_general(
            err_half, user_half, (((0,), (0,)), ((), ())), preferred_element_type=jnp.float32
        )
        * float(UT * TILE) ** (-0.5)
        + ridge_weight * item_fac
    )
    user_acc = user_acc + grad_user * grad_user
    item_acc = item_acc + grad_item * grad_item
    user_fac = user_fac - step_rate * grad_user * lax.rsqrt(user_acc)
    item_fac = item_fac - step_rate * grad_item * lax.rsqrt(item_acc)
    return (user_fac, user_acc, item_fac, item_acc, sq_error)


def on_device(ratings, tile_mask, tile_counts, users, user_accum, items, item_accum):
    strata_count = ratings.shape[0]
    slot_count = tile_mask.shape[1]
    tile_size = ratings.shape[1] // slot_count
    group_size = lax.axis_size("col")
    member = lax.axis_index("col")
    arrived_rows = users.shape[0]
    group_counts = lax.dynamic_slice_in_dim(
        tile_counts, lax.axis_index("row") * group_size, group_size
    )
    ranks = jnp.arange(group_size, dtype=jnp.int32)
    start_tile = jnp.sum(jnp.where(ranks < member, group_counts, 0))
    own_count = jnp.sum(jnp.where(ranks == member, group_counts, 0))
    valid = (jnp.arange(slot_count, dtype=jnp.int32) < own_count).astype(jnp.float32)
    whole_pair = lax.all_gather(jnp.stack([users, user_accum]), "col", axis=1, tiled=True)
    pad_rows = slot_count * tile_size
    ext_pair = jnp.concatenate([whole_pair, whole_pair[:, :pad_rows]], axis=1)
    user_pair = lax.dynamic_slice_in_dim(ext_pair, start_tile * tile_size, pad_rows, 1)
    user_fac = user_pair[0]
    user_acc = user_pair[1]
    held_pair = jnp.stack([items, item_accum])
    loss_list = []
    for stratum in range(strata_count):
        live_tiles = tile_mask[stratum].astype(jnp.float32) * valid[:, None]
        item_fac = held_pair[0]
        item_acc = held_pair[1]
        for inner in range(STEPS):
            user_fac, user_acc, item_fac, item_acc, sq_error = update(
                user_fac, user_acc, item_fac, item_acc, ratings[stratum], live_tiles
            )
            if inner == 0:
                observed = jnp.sum(live_tiles) * float(tile_size * tile_size)
                loss_list.append(jnp.stack([sq_error, observed]))
        held_pair = jnp.stack([item_fac, item_acc])
        if stratum + 1 < strata_count:
            held_pair = passed_along(held_pair, ("row", "col"), 1)
    loss_parts = lax.psum(jnp.stack(loss_list), ("row", "col"))
    losses = loss_parts[:, 0] / loss_parts[:, 1]
    row_valid = jnp.repeat(valid, tile_size)[None, :, None] > 0.5
    kept_pair = jnp.where(row_valid, jnp.stack([user_fac, user_acc]), 0.0)
    frame_rows = group_size * arrived_rows + pad_rows
    frame_pair = lax.dynamic_update_slice_in_dim(
        jnp.zeros((2, frame_rows, kept_pair.shape[2]), jnp.float32),
        kept_pair,
        start_tile * tile_size,
        1,
    )
    users_pair = lax.psum_scatter(
        frame_pair[:, : group_size * arrived_rows], "col", scatter_dimension=1, tiled=True
    )
    return (users_pair[0], users_pair[1], held_pair[0], held_pair[1], losses)


def solution(mesh):
    return jax.shard_map(
        on_device,
        mesh=mesh,
        in_specs=(
            P(None, ("row", "col"), None),
            P(None, ("row", "col"), None),
            P(),
            P(("row", "col"), None),
            P(("row", "col"), None),
            P(("row", "col"), None),
            P(("row", "col"), None),
        ),
        out_specs=(
            P(("row", "col"), None),
            P(("row", "col"), None),
            P(("row", "col"), None),
            P(("row", "col"), None),
            P(),
        ),
        check_vma=False,
    )
```

profile of v0, /device:TPU:1, one launch (start us, length us, event | category | flops | bytes accessed | tf_op | source)
XLA Modules:
  0.0 256.5 jit_solution(1015268047695154100)
XLA Ops:
  7.2 2.3 pad_maximum_fusion
  9.6 0.7 fusion.116
  11.0 0.7 compare_convert_fusion
  11.6 0.7 fusion.121
  12.4 39.6 %all-gather.2.cloned.1.call-done = f32[2,4096,128]{2,1,0:T(8,128)} async-done(((f32[2,1024,128]{2,1,0:T(8,128)}), f32[2,4096,128]{2,1,0:T(8,128)}) %all-gather.2.cloned.1.call-update) | async-done | bytes 4194320 | tf_op jit(solution)/shard_map/all_gather | solution.py:66
  51.9 1.9 slice.96
  53.8 2.2 fusion.32
  56.0 0.6 mul.537
  57.4 1.9 multiply_reduce_fusion.3
  59.3 0.7 multiply_subtract_fusion.10
  60.2 0.8 multiply_subtract_fusion.19
  61.0 0.7 fusion.1
  61.7 0.8 multiply_subtract_fusion.18
  62.5 1.7 multiply_subtract_fusion.9
  64.2 0.7 fusion.3
  64.9 0.8 subtract_bitcast_fusion.3
  65.7 0.8 pad_maximum_fusion.1
  66.6 2.6 %multiply_subtract_fusion.8 = (f32[2048,128]{1,0:T(8,128)S(1)}, f32[2048,128]{1,0:T(8,128)S(1)}) fusion(f32[2048,128]{1,0:T(8,128)S(1)} %get-tuple-element.57, f32[2048,128]{1,0:T(8,128)} %get-tuple-element.58, f32[2048,128]{1,0:T(8,128)} %copy-done.1, f32[2,2048,128]{2,1,0:T(8,128)} %copy-done, bf16[2048,512]{1,0:T(8,128)(2,1)S(1)} %fusion.3, ...), kind=kOutput, calls=%fused_computation.106 | convolution fusion | flops 271646720 | bytes 8650752 | tf_op jit(solution)/shard_map/dot_general | solution.py:34
  69.2 3.8 %collective-permute-done = f32[2,512,128]{2,1,0:T(8,128)} collective-permute-done((f32[2,512,128]{2,1,0:T(8,128)}, f32[2,512,128]{2,1,0:T(8,128)}, u32[]{:S(2)}, u32[]{:S(2)}) %collective-permute-start) | collective-permute-done | bytes 524320 | tf_op jit(solution)/shard_map/ppermute | solution.py:16
  73.0 0.6 mul.573
  73.6 3.7 %multiply_reduce_fusion.2 = (f32[]{:T(128)}, bf16[2048,512]{1,0:T(8,128)(2,1)S(1)}) fusion(f32[256,8,4,128]{3,2,1,0:T(4,128)S(1)} %bitcast.246, bf16[4,2048,512]{2,1,0:T(8,128)(2,1)} %param.7, f32[2,512,128]{2,1,0:T(8,128)} %collective-permute-done, f32[2048,128]{1,0:T(8,128)S(1)} %get-tuple-element.25), kind=kOutput, calls=%fused_computation.36 | convolution fusion | flops 274989056 | bytes 9568260 | tf_op jit(solution)/shard_map/dot_general | solution.py:23
  77.3 1.9 multiply_subtract_fusion.17
  79.3 1.7 multiply_subtract_fusion.7
  81.0 0.7 fusion.5
  81.7 1.7 multiply_subtract_fusion.6
  83.4 1.7 multiply_subtract_fusion.16
  85.1 0.7 fusion.7
  85.9 0.7 multiply_add_fusion.22
  86.6 1.0 subtract_bitcast_fusion.2
  87.7 0.8 pad_maximum_fusion.2
  88.5 4.0 %collective-permute-start.1 = (f32[2,512,128]{2,1,0:T(8,128)}, f32[2,512,128]{2,1,0:T(8,128)}, u32[]{:S(2)}, u32[]{:S(2)}) collective-permute-start(f32[2,512,128]{2,1,0:T(8,128)} %pad_maximum_fusion.2), channel_id=1, source_target_pairs={{0,1},{1,2},{2,3},{3,4},{4,5},{5,6},{6,7},{7,8},{8,9},{9,10},{10,1... | collective-permute-start | bytes 1572872 | tf_op jit(solution)/shard_map/ppermute | solution.py:16
  92.5 1.9 multiply_subtract_fusion.5
  94.5 4.4 %collective-permute-done.1 = f32[2,512,128]{2,1,0:T(8,128)} collective-permute-done((f32[2,512,128]{2,1,0:T(8,128)}, f32[2,512,128]{2,1,0:T(8,128)}, u32[]{:S(2)}, u32[]{:S(2)}) %collective-permute-start.1) | collective-permute-done | bytes 524320 | tf_op jit(solution)/shard_map/ppermute | solution.py:16
  99.5 3.7 %multiply_reduce_fusion.1 = (f32[]{:T(128)}, bf16[2048,512]{1,0:T(8,128)(2,1)S(1)}) fusion(f32[256,8,4,128]{3,2,1,0:T(4,128)S(1)} %bitcast.249, bf16[4,2048,512]{2,1,0:T(8,128)(2,1)} %param.7, f32[2,512,128]{2,1,0:T(8,128)} %collective-permute-done.1, f32[2048,128]{1,0:T(8,128)S(1)} %get-tuple-element.65), kind=kOutput, calls=%fused_computation.35 | convolution fusion | flops 274989056 | bytes 9568260 | tf_op jit(solution)/shard_map/dot_general | solution.py:23
  103.2 1.9 multiply_subtract_fusion.15
  105.2 1.7 multiply_subtract_fusion.4
  106.9 0.7 fusion.9
  107.8 1.8 multiply_subtract_fusion.3
  109.6 1.7 multiply_subtract_fusion.14
  111.3 0.7 fusion.11
  112.0 0.7 multiply_add_fusion.17
  112.8 1.0 subtract_bitcast_fusion.1
  113.8 0.8 pad_maximum_fusion.3
  114.6 4.0 %collective-permute-start.2 = (f32[2,512,128]{2,1,0:T(8,128)}, f32[2,512,128]{2,1,0:T(8,128)}, u32[]{:S(2)}, u32[]{:S(2)}) collective-permute-start(f32[2,512,128]{2,1,0:T(8,128)} %pad_maximum_fusion.3), channel_id=1, source_target_pairs={{0,1},{1,2},{2,3},{3,4},{4,5},{5,6},{6,7},{7,8},{8,9},{9,10},{10,1... | collective-permute-start | bytes 1572872 | tf_op jit(solution)/shard_map/ppermute | solution.py:16
  118.8 2.3 multiply_subtract_fusion.2
  121.1 7.4 %collective-permute-done.2 = f32[2,512,128]{2,1,0:T(8,128)} collective-permute-done((f32[2,512,128]{2,1,0:T(8,128)}, f32[2,512,128]{2,1,0:T(8,128)}, u32[]{:S(2)}, u32[]{:S(2)}) %collective-permute-start.2) | collective-permute-done | bytes 524320 | tf_op jit(solution)/shard_map/ppermute | solution.py:16
  128.5 0.6 mul.645
  129.1 3.7 %multiply_reduce_fusion = (f32[]{:T(128)}, bf16[2048,512]{1,0:T(8,128)(2,1)S(1)}) fusion(f32[256,8,4,128]{3,2,1,0:T(4,128)S(1)} %bitcast.252, bf16[4,2048,512]{2,1,0:T(8,128)(2,1)} %param.7, f32[2,512,128]{2,1,0:T(8,128)} %collective-permute-done.2, f32[2048,128]{1,0:T(8,128)S(1)} %get-tuple-element.19), kind=kOutput, calls=%fused_computation.34 | convolution fusion | flops 274989056 | bytes 9568260 | tf_op jit(solution)/shard_map/dot_general | solution.py:23
  132.8 1.9 multiply_subtract_fusion.13
  134.8 1.8 multiply_subtract_fusion.1
  136.6 0.7 fusion.13
  137.3 0.8 multiply_subtract_fusion
  138.0 2.4 multiply_subtract_fusion.12
  140.5 0.7 fusion.15
  141.2 0.7 subtract_bitcast_fusion
  142.8 2.2 slice.105
  147.6 0.7 maximum_bitcast_fusion
  148.3 0.7 maximum_bitcast_fusion.1
  149.0 0.6 maximum_bitcast_fusion.2
  149.6 0.7 maximum_bitcast_fusion.3
  150.4 93.7 %psum.7 = f32[4,2]{1,0:T(4,128)S(1)} all-reduce(f32[4,2]{1,0:T(4,128)S(1)} %pad_maximum_fusion.4), channel_id=1, replica_groups=mesh['row'=32,'col'=4] {'row','col'}, use_global_device_ids=true, to_apply=%region_11.12 | all-reduce | flops 8 | bytes 64 | tf_op jit(solution)/shard_map/psum | solution.py:88
  244.1 0.7 fusion.115
  244.8 2.6 %multiply_subtract_fusion.11 = (f32[512,128]{1,0:T(8,128)}, f32[512,128]{1,0:T(8,128)}) fusion(f32[512,128]{1,0:T(8,128)S(1)} %get-tuple-element.77, f32[512,128]{1,0:T(8,128)} %get-tuple-element.78, f32[512,128]{1,0:T(8,128)} %copy-done.4, f32[2,512,128]{2,1,0:T(8,128)} %collective-permute-done.2, bf16[2048,512]{1,0:T(8,128)(2,1)S(1)} %fusion.15, ...), kind=kOutput, calls=%fused_computation.127 | convolution fusion | flops 269484032 | bytes 4718592 | tf_op jit(solution)/shard_map/dot_general | solution.py:39
  247.4 2.2 slice_bitcast_fusion.2
  (53 shorter events, 3.2 us)
Async XLA Ops:
  7.2 2.4 copy-start.8
  7.2 4.4 %copy-start.7 = (s32[4,16,4]{1,2,0:T(4,128)S(1)}, s32[4,16,4]{1,2,0:T(4,128)}, u32[]{:S(2)}) copy-start(s32[4,16,4]{1,2,0:T(4,128)} %param.8) | copy-start | bytes 3076
  7.2 44.8 %all-gather.2.cloned.1.call-start = ((), (), s32[]{:S(2)}) async-start(), calls=%async_computation.1 | async-start | bytes 5242880 | tf_op jit(solution)/shard_map/all_gather | solution.py:66
  9.5 237.9 %reduce-scatter.2.cloned.1.call-start = ((), (), s32[]{:S(2)}) async-start(), calls=%async_computation.2 | async-start | bytes 5242880 | tf_op jit(solution)/shard_map/reduce_scatter | solution.py:99
  51.9 4.7 %slice-start = ((s8[8388608]{0:T(1024)(128)(4,1)}), s8[4194304]{0:T(1024)(128)(4,1)S(1)}, s32[]{:S(2)}) async-start(s8[8388608]{0:T(1024)(128)(4,1)} %bitcast.238), calls=%async_computation.3 | async-start | bytes 8388608
  53.8 3.1 %slice-start.1 = ((s8[8388608]{0:T(1024)(128)(4,1)}), s8[4194304]{0:T(1024)(128)(4,1)S(1)}, s32[]{:S(2)}) async-start(s8[8388608]{0:T(1024)(128)(4,1)} %bitcast.238), calls=%async_computation.4 | async-start | bytes 8388608
  56.0 6.5 %copy-start = (f32[2,2048,128]{2,1,0:T(8,128)}, f32[2,2048,128]{2,1,0:T(8,128)S(1)}, u32[]{:S(2)}) copy-start(f32[2,2048,128]{2,1,0:T(8,128)S(1)} %fusion.32) | copy-start | bytes 6291460
  56.0 1.4 copy-start.5
  59.3 0.9 copy-start.6
  60.2 2.3 copy-start.1
  66.5 6.4 %collective-permute-start = (f32[2,512,128]{2,1,0:T(8,128)}, f32[2,512,128]{2,1,0:T(8,128)}, u32[]{:S(2)}, u32[]{:S(2)}) collective-permute-start(f32[2,512,128]{2,1,0:T(8,128)} %pad_maximum_fusion.1), channel_id=1, source_target_pairs={{0,1},{1,2},{2,3},{3,4},{4,5},{5,6},{6,7},{7,8},{8,9},{9,10},{10,1... | collective-permute-start | bytes 1572872 | tf_op jit(solution)/shard_map/ppermute | solution.py:16
  73.6 7.4 %slice-start.2 = ((s8[8388608]{0:T(1024)(128)(4,1)}), s8[4194304]{0:T(1024)(128)(4,1)S(1)}, s32[]{:S(2)}) async-start(s8[8388608]{0:T(1024)(128)(4,1)} %bitcast.240), calls=%async_computation.5 | async-start | bytes 8388608
  77.3 3.6 %slice-start.3 = ((s8[8388608]{0:T(1024)(128)(4,1)}), s8[4194304]{0:T(1024)(128)(4,1)S(1)}, s32[]{:S(2)}) async-start(s8[8388608]{0:T(1024)(128)(4,1)} %bitcast.240), calls=%async_computation.6 | async-start | bytes 8388608
  88.5 10.4 %collective-permute-start.1 = (f32[2,512,128]{2,1,0:T(8,128)}, f32[2,512,128]{2,1,0:T(8,128)}, u32[]{:S(2)}, u32[]{:S(2)}) collective-permute-start(f32[2,512,128]{2,1,0:T(8,128)} %pad_maximum_fusion.2), channel_id=1, source_target_pairs={{0,1},{1,2},{2,3},{3,4},{4,5},{5,6},{6,7},{7,8},{8,9},{9,10},{10,1... | collective-permute-start | bytes 1572872 | tf_op jit(solution)/shard_map/ppermute | solution.py:16
  99.5 7.4 %slice-start.4 = ((s8[8388608]{0:T(1024)(128)(4,1)}), s8[4194304]{0:T(1024)(128)(4,1)S(1)}, s32[]{:S(2)}) async-start(s8[8388608]{0:T(1024)(128)(4,1)} %bitcast.242), calls=%async_computation.7 | async-start | bytes 8388608
  103.2 1.9 copy-start.2
  103.2 3.7 %slice-start.5 = ((s8[8388608]{0:T(1024)(128)(4,1)}), s8[4194304]{0:T(1024)(128)(4,1)S(1)}, s32[]{:S(2)}) async-start(s8[8388608]{0:T(1024)(128)(4,1)} %bitcast.242), calls=%async_computation.8 | async-start | bytes 8388608
  106.9 0.9 copy-start.3
  114.6 13.9 %collective-permute-start.2 = (f32[2,512,128]{2,1,0:T(8,128)}, f32[2,512,128]{2,1,0:T(8,128)}, u32[]{:S(2)}, u32[]{:S(2)}) collective-permute-start(f32[2,512,128]{2,1,0:T(8,128)} %pad_maximum_fusion.3), channel_id=1, source_target_pairs={{0,1},{1,2},{2,3},{3,4},{4,5},{5,6},{6,7},{7,8},{8,9},{9,10},{10,1... | collective-permute-start | bytes 1572872 | tf_op jit(solution)/shard_map/ppermute | solution.py:16
  129.1 7.4 %slice-start.6 = ((s8[8388608]{0:T(1024)(128)(4,1)}), s8[4194304]{0:T(1024)(128)(4,1)S(1)}, s32[]{:S(2)}) async-start(s8[8388608]{0:T(1024)(128)(4,1)} %bitcast.244), calls=%async_computation.9 | async-start | bytes 8388608
  132.8 3.7 %slice-start.7 = ((s8[8388608]{0:T(1024)(128)(4,1)}), s8[4194304]{0:T(1024)(128)(4,1)S(1)}, s32[]{:S(2)}) async-start(s8[8388608]{0:T(1024)(128)(4,1)} %bitcast.244), calls=%async_computation.10 | async-start | bytes 8388608
  134.7 3.3 %copy-start.4 = (f32[512,128]{1,0:T(8,128)}, f32[512,128]{1,0:T(8,128)S(1)}, u32[]{:S(2)}) copy-start(f32[512,128]{1,0:T(8,128)S(1)} %get-tuple-element.76) | copy-start | bytes 786436
Sparse Core Ops, SparseCore 0:
  9.7 42.2 all-gather.1
  145.1 56.8 reduce-scatter.1
where the time goes:
time: 257 us
  blocking collectives  93.7 us (36%)
  matrix products  56 us (22%)
  waiting for transfers between devices  55.2 us (21%)
  between operations  17.7 us (7%)
  other arithmetic  15 us (6%)
  local copies, waits for them, and re-layouts  10.8 us (4%)
  starting transfers between devices  8.05 us (3%)
    psum x1, blocking collectives, on_device(): loss_parts = lax.psum(jnp.stack(loss_list), ('row', 'col'))  93.7 us
    all_gather x1, waiting for transfers between devices, on_device(): lax.all_gather(jnp.stack([users, user_accum]), 'col', axis=1, tiled=True)  39.6 us
    dot_general x12, matrix products, update(): jnp.dot(err_half, item_half, preferred_element_type=jnp.float32)  19.3 us
    dot_general x12, matrix products, update(): lax.dot_general(user_half, item_half, (((1,), (1,)), ((), ())), preferred...  18.7 us
    dot_general x12, matrix products, update(): lax.dot_general(err_half, user_half, (((0,), (0,)), ((), ())), preferred_...  18.1 us
    ppermute x3, waiting for transfers between devices, passed_along(): return lax.ppermute(value, axis, pairs)  15.6 us
    ppermute x3, starting transfers between devices, passed_along(): return lax.ppermute(value, axis, pairs)  7.97 us
  transfers between devices with their start and end apart: 5, of which 4 were waited for; matrix products, arithmetic and copies ran while one was open for 6% of the time, Pallas kernels for 0%

commit v1 on v0

--- a/solution.py
+++ b/solution.py
@@ -2,12 +2,18 @@
 import jax.numpy as jnp
 from jax import lax
 from jax.sharding import PartitionSpec as P
+from jax.lax import all_to_all, axis_size
 
 TILE = 128
 UT = 8
 STEPS = 3
 ridge_weight = 0.02
 step_rate = 0.05
+
+
+def number_series(message):
+    r1 = jnp.concatenate(all_to_all(jnp.stack(axis_size("col") * [message], 0), "col", 0, 0), 1)
+    return r1
 
 
 def passed_along(value, axis, steps):
@@ -63,7 +69,7 @@
     start_tile = jnp.sum(jnp.where(ranks < member, group_counts, 0))
     own_count = jnp.sum(jnp.where(ranks == member, group_counts, 0))
     valid = (jnp.arange(slot_count, dtype=jnp.int32) < own_count).astype(jnp.float32)
-    whole_pair = lax.all_gather(jnp.stack([users, user_accum]), "col", axis=1, tiled=True)
+    whole_pair = number_series(jnp.stack([users, user_accum]))
     pad_rows = slot_count * tile_size
     ext_pair = jnp.concatenate([whole_pair, whole_pair[:, :pad_rows]], axis=1)
     user_pair = lax.dynamic_slice_in_dim(ext_pair, start_tile * tile_size, pad_rows, 1)

time: 257 us -> 276 us (1.074)
  starting transfers between devices: 8.05 us -> 15.7 us
  waiting for transfers between devices: 55.2 us -> 61.3 us
  local copies, waits for them, and re-layouts: 10.8 us -> 15.9 us
    all_to_all x0 -> x1, waiting for transfers between devices: none -> 45.9 us  [number_series(): all_to_all(jnp.stack(axis_size('col') * [message], 0), 'col', 0, 0)]
    all_gather x1 -> x0, waiting for transfers between devices: 39.6 us -> none  [on_device(): lax.all_gather(jnp.stack([users, user_accum]), 'col', axis=1, tiled=True)]
    all_to_all x0 -> x1, starting transfers between devices: none -> 6.77 us  [number_series(): all_to_all(jnp.stack(axis_size('col') * [message], 0), 'col', 0, 0)]
where the time goes in v1:
time: 276 us; the launch traced here: 275 us
  blocking collectives  96 us (35%)
  waiting for transfers between devices  61.3 us (22%)
  matrix products  56.1 us (20%)
  between operations  17.8 us (6%)
  local copies, waits for them, and re-layouts  15.9 us (6%)
  starting transfers between devices  15.7 us (6%)
  other arithmetic  12.6 us (5%)
    psum x1, blocking collectives, on_device(): loss_parts = lax.psum(jnp.stack(loss_list), ('row', 'col'))  96 us
    all_to_all x1, waiting for transfers between devices, number_series(): all_to_all(jnp.stack(axis_size('col') * [message], 0), 'col', 0, 0)  45.9 us
    dot_general x12, matrix products, update(): jnp.dot(err_half, item_half, preferred_element_type=jnp.float32)  19.3 us
    dot_general x12, matrix products, update(): lax.dot_general(user_half, item_half, (((1,), (1,)), ((), ())), preferred...  18.7 us
    dot_general x12, matrix products, update(): lax.dot_general(err_half, user_half, (((0,), (0,)), ((), ())), preferred_...  18.1 us
    ppermute x3, waiting for transfers between devices, passed_along(): return lax.ppermute(value, axis, pairs)  15.4 us
    ppermute x3, starting transfers between devices, passed_along(): return lax.ppermute(value, axis, pairs)  8.96 us
    all_to_all x1, starting transfers between devices, number_series(): all_to_all(jnp.stack(axis_size('col') * [message], 0), 'col', 0, 0)  6.77 us
  transfers between devices with their start and end apart: 5, of which 4 were waited for; matrix products, arithmetic and copies ran while one was open for 6% of the time, Pallas kernels for 0%

profile of v1, /device:TPU:1, one launch (start us, length us, event | category | flops | bytes accessed | tf_op | source)
XLA Modules:
  0.0 275.4 jit_solution(10104780398952972332)
XLA Ops:
  7.2 1.3 pad_maximum_fusion
  8.4 2.3 stack.106
  10.7 6.8 %all-to-all-start = ((f32[4,2,1024,128]{3,2,1,0:T(8,128)}), f32[4,2,1024,128]{3,2,1,0:T(8,128)}, u32[]{:S(2)}, u32[]{:S(2)}) async-start(f32[4,2,1024,128]{3,2,1,0:T(8,128)} %stack.106), calls=%async_computation | async-start | bytes 8388608 | tf_op jit(solution)/shard_map/all_to_all | solution.py:15
  17.5 0.7 fusion.116
  19.5 0.7 fusion.121
  20.3 45.9 %all-to-all-done = f32[4,2,1024,128]{3,2,1,0:T(8,128)} async-done(((f32[4,2,1024,128]{3,2,1,0:T(8,128)}), f32[4,2,1024,128]{3,2,1,0:T(8,128)}, u32[]{:S(2)}, u32[]{:S(2)}) %all-to-all-start) | async-done | bytes 4194336 | tf_op jit(solution)/shard_map/all_to_all | solution.py:15
  66.3 2.5 copy.20
  70.2 1.5 slice-done
  71.7 1.3 slice-done.1
  73.0 1.9 multiply_reduce_fusion.3
  74.9 0.7 multiply_subtract_fusion.10
  75.9 0.8 multiply_subtract_fusion.19
  76.6 0.7 fusion.1
  77.4 0.8 multiply_subtract_fusion.18
  78.2 1.7 multiply_subtract_fusion.9
  79.9 0.7 fusion.3
  80.6 0.8 subtract_bitcast_fusion.3
  81.3 0.8 pad_maximum_fusion.1
  82.2 1.0 collective-permute-start
  83.3 2.6 multiply_subtract_fusion.8
  85.8 3.8 %collective-permute-done = f32[2,512,128]{2,1,0:T(8,128)} collective-permute-done((f32[2,512,128]{2,1,0:T(8,128)}, f32[2,512,128]{2,1,0:T(8,128)}, u32[]{:S(2)}, u32[]{:S(2)}) %collective-permute-start) | collective-permute-done | bytes 524320 | tf_op jit(solution)/shard_map/ppermute | solution.py:22
  90.2 3.7 %multiply_reduce_fusion.2 = (f32[]{:T(128)}, bf16[2048,512]{1,0:T(8,128)(2,1)S(1)}) fusion(f32[256,8,4,128]{3,2,1,0:T(4,128)S(1)} %bitcast.248, bf16[4,2048,512]{2,1,0:T(8,128)(2,1)} %param.7, f32[2,512,128]{2,1,0:T(8,128)} %collective-permute-done, f32[2048,128]{1,0:T(8,128)S(1)} %get-tuple-element.25), kind=kOutput, calls=%fused_computation.36 | convolution fusion | flops 274989056 | bytes 9568260 | tf_op jit(solution)/shard_map/dot_general | solution.py:29
  93.9 1.9 multiply_subtract_fusion.17
  95.9 1.7 multiply_subtract_fusion.7
  97.6 0.7 fusion.5
  98.3 1.7 multiply_subtract_fusion.6
  100.0 1.7 multiply_subtract_fusion.16
  101.8 0.7 fusion.7
  102.5 0.7 multiply_add_fusion.22
  103.2 1.0 subtract_bitcast_fusion.2
  104.3 0.8 pad_maximum_fusion.2
  105.1 4.0 %collective-permute-start.1 = (f32[2,512,128]{2,1,0:T(8,128)}, f32[2,512,128]{2,1,0:T(8,128)}, u32[]{:S(2)}, u32[]{:S(2)}) collective-permute-start(f32[2,512,128]{2,1,0:T(8,128)} %pad_maximum_fusion.2), channel_id=1, source_target_pairs={{0,1},{1,2},{2,3},{3,4},{4,5},{5,6},{6,7},{7,8},{8,9},{9,10},{10,1... | collective-permute-start | bytes 1572872 | tf_op jit(solution)/shard_map/ppermute | solution.py:22
  109.2 1.9 multiply_subtract_fusion.5
  111.1 4.4 %collective-permute-done.1 = f32[2,512,128]{2,1,0:T(8,128)} collective-permute-done((f32[2,512,128]{2,1,0:T(8,128)}, f32[2,512,128]{2,1,0:T(8,128)}, u32[]{:S(2)}, u32[]{:S(2)}) %collective-permute-start.1) | collective-permute-done | bytes 524320 | tf_op jit(solution)/shard_map/ppermute | solution.py:22
  116.2 3.7 %multiply_reduce_fusion.1 = (f32[]{:T(128)}, bf16[2048,512]{1,0:T(8,128)(2,1)S(1)}) fusion(f32[256,8,4,128]{3,2,1,0:T(4,128)S(1)} %bitcast.251, bf16[4,2048,512]{2,1,0:T(8,128)(2,1)} %param.7, f32[2,512,128]{2,1,0:T(8,128)} %collective-permute-done.1, f32[2048,128]{1,0:T(8,128)S(1)} %get-tuple-element.65), kind=kOutput, calls=%fused_computation.35 | convolution fusion | flops 274989056 | bytes 9568260 | tf_op jit(solution)/shard_map/dot_general | solution.py:29
  119.9 1.9 multiply_subtract_fusion.15
  121.9 1.7 multiply_subtract_fusion.4
  123.6 0.7 fusion.9
  124.5 1.8 multiply_subtract_fusion.3
  126.3 1.7 multiply_subtract_fusion.14
  128.0 0.7 fusion.11
  128.7 0.7 multiply_add_fusion.17
  129.5 1.0 subtract_bitcast_fusion.1
  130.5 0.8 pad_maximum_fusion.3
  131.4 4.0 %collective-permute-start.2 = (f32[2,512,128]{2,1,0:T(8,128)}, f32[2,512,128]{2,1,0:T(8,128)}, u32[]{:S(2)}, u32[]{:S(2)}) collective-permute-start(f32[2,512,128]{2,1,0:T(8,128)} %pad_maximum_fusion.3), channel_id=1, source_target_pairs={{0,1},{1,2},{2,3},{3,4},{4,5},{5,6},{6,7},{7,8},{8,9},{9,10},{10,1... | collective-permute-start | bytes 1572872 | tf_op jit(solution)/shard_map/ppermute | solution.py:22
  135.5 2.3 multiply_subtract_fusion.2
  137.8 7.2 %collective-permute-done.2 = f32[2,512,128]{2,1,0:T(8,128)} collective-permute-done((f32[2,512,128]{2,1,0:T(8,128)}, f32[2,512,128]{2,1,0:T(8,128)}, u32[]{:S(2)}, u32[]{:S(2)}) %collective-permute-start.2) | collective-permute-done | bytes 524320 | tf_op jit(solution)/shard_map/ppermute | solution.py:22
  145.6 3.7 %multiply_reduce_fusion = (f32[]{:T(128)}, bf16[2048,512]{1,0:T(8,128)(2,1)S(1)}) fusion(f32[256,8,4,128]{3,2,1,0:T(4,128)S(1)} %bitcast.254, bf16[4,2048,512]{2,1,0:T(8,128)(2,1)} %param.7, f32[2,512,128]{2,1,0:T(8,128)} %collective-permute-done.2, f32[2048,128]{1,0:T(8,128)S(1)} %get-tuple-element.19), kind=kOutput, calls=%fused_computation.34 | convolution fusion | flops 274989056 | bytes 9568260 | tf_op jit(solution)/shard_map/dot_general | solution.py:29
  149.2 1.9 multiply_subtract_fusion.13
  151.2 1.8 multiply_subtract_fusion.1
  153.0 0.7 fusion.13
  153.7 0.8 multiply_subtract_fusion
  154.5 2.4 multiply_subtract_fusion.12
  156.9 0.7 fusion.15
  157.6 0.7 subtract_bitcast_fusion
  159.2 2.2 slice.105
  164.1 0.7 maximum_bitcast_fusion
  164.8 0.7 maximum_bitcast_fusion.1
  165.5 0.7 maximum_bitcast_fusion.2
  166.2 0.7 maximum_bitcast_fusion.3
  167.0 96.0 %psum.7 = f32[4,2]{1,0:T(4,128)S(1)} all-reduce(f32[4,2]{1,0:T(4,128)S(1)} %pad_maximum_fusion.4), channel_id=1, replica_groups=mesh['row'=32,'col'=4] {'row','col'}, use_global_device_ids=true, to_apply=%region_11.12 | all-reduce | flops 8 | bytes 64 | tf_op jit(solution)/shard_map/psum | solution.py:94
  263.0 0.7 fusion.115
  263.7 2.6 multiply_subtract_fusion.11
  266.3 2.2 slice_bitcast_fusion.2
  (54 shorter events, 5.6 us)
Async XLA Ops:
  10.7 6.8 %copy-start.8 = (s32[128]{0:T(128)S(1)}, s32[128]{0:T(128)}, u32[]{:S(2)}) copy-start(s32[128]{0:T(128)} %param.9) | copy-start | bytes 1540
  10.7 8.8 %copy-start.7 = (s32[4,16,4]{1,2,0:T(4,128)S(1)}, s32[4,16,4]{1,2,0:T(4,128)}, u32[]{:S(2)}) copy-start(s32[4,16,4]{1,2,0:T(4,128)} %param.8) | copy-start | bytes 3076
  10.7 55.5 %all-to-all-start = ((f32[4,2,1024,128]{3,2,1,0:T(8,128)}), f32[4,2,1024,128]{3,2,1,0:T(8,128)}, u32[]{:S(2)}, u32[]{:S(2)}) async-start(f32[4,2,1024,128]{3,2,1,0:T(8,128)} %stack.106), calls=%async_computation | async-start | bytes 8388608 | tf_op jit(solution)/shard_map/all_to_all | solution.py:15
  17.5 248.8 %reduce-scatter.2.cloned.1.call-start = ((), (), s32[]{:S(2)}) async-start(), calls=%async_computation.2 | async-start | bytes 5242880 | tf_op jit(solution)/shard_map/reduce_scatter | solution.py:105
  68.7 2.9 %slice-start = ((s8[8388608]{0:T(1024)(128)(4,1)}), s8[4194304]{0:T(1024)(128)(4,1)S(1)}, s32[]{:S(2)}) async-start(s8[8388608]{0:T(1024)(128)(4,1)} %bitcast.240), calls=%async_computation.3 | async-start | bytes 8388608
  68.9 4.1 %slice-start.1 = ((s8[8388608]{0:T(1024)(128)(4,1)}), s8[4194304]{0:T(1024)(128)(4,1)S(1)}, s32[]{:S(2)}) async-start(s8[8388608]{0:T(1024)(128)(4,1)} %bitcast.240), calls=%async_computation.4 | async-start | bytes 8388608
  69.5 8.6 %copy-start = (f32[2,2048,128]{2,1,0:T(8,128)}, f32[2,2048,128]{2,1,0:T(8,128)S(1)}, u32[]{:S(2)}) copy-start(f32[2,2048,128]{2,1,0:T(8,128)S(1)} %fusion.32) | copy-start | bytes 6291460
  69.6 3.5 %copy-start.5 = (f32[512,128]{1,0:T(8,128)S(1)}, f32[512,128]{1,0:T(8,128)}, u32[]{:S(2)}) copy-start(f32[512,128]{1,0:T(8,128)} %param.12) | copy-start | bytes 786436
  74.9 0.9 copy-start.6
  75.9 2.3 copy-start.1
  82.2 7.4 %collective-permute-start = (f32[2,512,128]{2,1,0:T(8,128)}, f32[2,512,128]{2,1,0:T(8,128)}, u32[]{:S(2)}, u32[]{:S(2)}) collective-permute-start(f32[2,512,128]{2,1,0:T(8,128)} %pad_maximum_fusion.1), channel_id=1, source_target_pairs={{0,1},{1,2},{2,3},{3,4},{4,5},{5,6},{6,7},{7,8},{8,9},{9,10},{10,1... | collective-permute-start | bytes 1572872 | tf_op jit(solution)/shard_map/ppermute | solution.py:22
  90.2 7.3 %slice-start.2 = ((s8[8388608]{0:T(1024)(128)(4,1)}), s8[4194304]{0:T(1024)(128)(4,1)S(1)}, s32[]{:S(2)}) async-start(s8[8388608]{0:T(1024)(128)(4,1)} %bitcast.242), calls=%async_computation.5 | async-start | bytes 8388608
  93.9 3.6 %slice-start.3 = ((s8[8388608]{0:T(1024)(128)(4,1)}), s8[4194304]{0:T(1024)(128)(4,1)S(1)}, s32[]{:S(2)}) async-start(s8[8388608]{0:T(1024)(128)(4,1)} %bitcast.242), calls=%async_computation.6 | async-start | bytes 8388608
  105.1 10.4 %collective-permute-start.1 = (f32[2,512,128]{2,1,0:T(8,128)}, f32[2,512,128]{2,1,0:T(8,128)}, u32[]{:S(2)}, u32[]{:S(2)}) collective-permute-start(f32[2,512,128]{2,1,0:T(8,128)} %pad_maximum_fusion.2), channel_id=1, source_target_pairs={{0,1},{1,2},{2,3},{3,4},{4,5},{5,6},{6,7},{7,8},{8,9},{9,10},{10,1... | collective-permute-start | bytes 1572872 | tf_op jit(solution)/shard_map/ppermute | solution.py:22
  116.1 7.4 %slice-start.4 = ((s8[8388608]{0:T(1024)(128)(4,1)}), s8[4194304]{0:T(1024)(128)(4,1)S(1)}, s32[]{:S(2)}) async-start(s8[8388608]{0:T(1024)(128)(4,1)} %bitcast.244), calls=%async_computation.7 | async-start | bytes 8388608
  119.9 1.9 copy-start.2
  119.9 3.7 %slice-start.5 = ((s8[8388608]{0:T(1024)(128)(4,1)}), s8[4194304]{0:T(1024)(128)(4,1)S(1)}, s32[]{:S(2)}) async-start(s8[8388608]{0:T(1024)(128)(4,1)} %bitcast.244), calls=%async_computation.8 | async-start | bytes 8388608
  123.5 1.0 copy-start.3
  131.4 13.6 %collective-permute-start.2 = (f32[2,512,128]{2,1,0:T(8,128)}, f32[2,512,128]{2,1,0:T(8,128)}, u32[]{:S(2)}, u32[]{:S(2)}) collective-permute-start(f32[2,512,128]{2,1,0:T(8,128)} %pad_maximum_fusion.3), channel_id=1, source_target_pairs={{0,1},{1,2},{2,3},{3,4},{4,5},{5,6},{6,7},{7,8},{8,9},{9,10},{10,1... | collective-permute-start | bytes 1572872 | tf_op jit(solution)/shard_map/ppermute | solution.py:22
  145.6 7.4 %slice-start.6 = ((s8[8388608]{0:T(1024)(128)(4,1)}), s8[4194304]{0:T(1024)(128)(4,1)S(1)}, s32[]{:S(2)}) async-start(s8[8388608]{0:T(1024)(128)(4,1)} %bitcast.246), calls=%async_computation.9 | async-start | bytes 8388608
  149.2 3.7 %slice-start.7 = ((s8[8388608]{0:T(1024)(128)(4,1)}), s8[4194304]{0:T(1024)(128)(4,1)S(1)}, s32[]{:S(2)}) async-start(s8[8388608]{0:T(1024)(128)(4,1)} %bitcast.246), calls=%async_computation.10 | async-start | bytes 8388608
  151.2 3.3 %copy-start.4 = (f32[512,128]{1,0:T(8,128)}, f32[512,128]{1,0:T(8,128)S(1)}, u32[]{:S(2)}) copy-start(f32[512,128]{1,0:T(8,128)S(1)} %get-tuple-element.76) | copy-start | bytes 786436
Sparse Core Ops, SparseCore 0:
  161.6 56.8 reduce-scatter.1
